TPU v7x, 32 devices: a whole 2x2x4 slice. The times are simulated.
32 devices in a mesh: row: 8 (over z, y), col: 4 (over x, core).
Axes of the slice: x: 2, y: 2, z: 4, core: 2. Of those that a mesh axis runs over, the one named last changes fastest.
Arguments:
- x_t: bfloat16 [128, 8192], P('col', 'row'), may hold values from -6 to 6
- tiles: bfloat16 [64, 128, 128], P('row'), may hold values from -0.375 to 0.375
- tile_owner: int32 [64, 1], P('row'), may hold values from 0 to 7; in each aligned block of 8 rows (0 to 7, 8 to 15, ...) at most 2 rows name the same one
- tile_local: int32 [64, 2], P('row'), may hold values from 0 to 7
- weight: bfloat16 [128, 256], replicated, may hold values from -0.5 to 0.5
- cotangent: bfloat16 [8192, 256], P('row'), may hold values from -0.0625 to 0.0625
Outputs:
- act: bfloat16 [8192, 256], P('row')
- grad_w: float32 [128, 256], P('col')
Inputs may be any that keep to these rules, and one draw needn't show every extreme that they name: `tile_owner`: within the 8 stored tiles of one index of row (aligned blocks of 8 rows) no owner appears more than 2 times, and some owner appears exactly 2 times.
All inputs are finite; a program needn't handle non-finite values.
Results may differ from a plain program's by a relative error of at most 0.0059.
Values may be sent and summed in bfloat16 or wider, within the bound.
No kernel may reach another device: no remote copies, remote signals or barrier semaphores. Data moves between devices by JAX's collectives and lax.ppermute only.
A program may use at most 64 MiB of HBM per device.

v0:
```python
import jax
import jax.numpy as jnp
from jax import lax
from jax.sharding import PartitionSpec as P


def gather_groups(z_part, n_col):
    if n_col == 1:
        return z_part
    me = lax.axis_index("col")
    parts = [z_part]
    for k in range(1, n_col):
        perm = [(i, (i + k) % n_col) for i in range(n_col)]
        parts.append(lax.ppermute(z_part, "col", perm))
    stacked = jnp.stack(parts)
    order = (me - jnp.arange(n_col, dtype=jnp.int32)) % n_col
    full = jnp.take(stacked, order, axis=0)
    return full.reshape(n_col * z_part.shape[0], z_part.shape[1])


def sum_over_row(x, n_row):
    if n_row & n_row - 1:
        return lax.psum(x, "row")
    k = 1
    while k < n_row:
        perm = [(i, i ^ k) for i in range(n_row)]
        x = x + lax.ppermute(x, "row", perm)
        k *= 2
    return x


def body(x_t, tiles, tile_owner, tile_local, weight, cotangent):
    n_row = lax.axis_size("row")
    n_col = lax.axis_size("col")
    n_tiles, tile_dim = (tiles.shape[0], tiles.shape[1])
    feat_q, rows = x_t.shape
    n_blocks = rows // tile_dim
    capacity = 2 * (n_tiles // n_row)
    xb = x_t.reshape(feat_q, n_blocks, tile_dim).transpose(1, 0, 2)
    flat_blocks = xb.reshape(n_blocks, feat_q * tile_dim)
    owner = tile_owner[:, 0]
    row_local = tile_local[:, 0]
    col_local = tile_local[:, 1]
    owner_hot = (owner[:, None] == jnp.arange(n_row, dtype=jnp.int32)[None, :]).astype(jnp.int32)
    rank = jnp.sum(owner_hot * (jnp.cumsum(owner_hot, axis=0) - 1), axis=1)
    slot = owner * capacity + rank
    slot_ids = (
        jnp.zeros((n_row * capacity,), jnp.int32).at[slot].set(col_local).reshape(n_row, capacity)
    )
    id_rows = jnp.zeros((n_row, 1, feat_q * tile_dim), jnp.bfloat16)
    id_rows = id_rows.at[:, 0, :capacity].set(slot_ids.astype(jnp.bfloat16))
    own_blocks = jnp.take(xb, row_local, axis=0)
    mirror_terms = jnp.einsum(
        "tfi,tij->tfj", own_blocks, tiles, preferred_element_type=jnp.float32
    ).astype(jnp.bfloat16)
    outgoing = jnp.zeros((n_row * capacity, feat_q * tile_dim), jnp.bfloat16)
    outgoing = (
        outgoing.at[slot]
        .set(mirror_terms.reshape(n_tiles, feat_q * tile_dim))
        .reshape(n_row, capacity, feat_q * tile_dim)
    )
    every_block = jnp.broadcast_to(flat_blocks[None], (n_row, n_blocks, feat_q * tile_dim))
    payload = jnp.concatenate([every_block, outgoing, id_rows], axis=1)
    got = lax.all_to_all(payload, "row", split_axis=0, concat_axis=0, tiled=True)
    all_x = got[:, :n_blocks].reshape(n_row * n_blocks, feat_q, tile_dim)
    incoming = got[:, n_blocks : n_blocks + capacity]
    block_ids = got[:, n_blocks + capacity, :capacity].astype(jnp.int32)
    fetched_tiles = jnp.take(all_x, owner * n_blocks + col_local, axis=0)
    forward_terms = jnp.einsum(
        "tfj,tij->tfi", fetched_tiles, tiles, preferred_element_type=jnp.float32
    )
    block_range = jnp.arange(n_blocks, dtype=jnp.int32)
    row_hot = (row_local[:, None] == block_range[None, :]).astype(jnp.float32)
    local_sum = jnp.einsum("tfi,tb->fbi", forward_terms, row_hot, precision=lax.Precision.HIGHEST)
    in_hot = (block_ids.reshape(-1)[:, None] == block_range[None, :]).astype(jnp.bfloat16)
    mirror_sum = jnp.einsum(
        "sk,sb->bk",
        incoming.reshape(n_row * capacity, feat_q * tile_dim),
        in_hot,
        preferred_element_type=jnp.float32,
    )
    mirror_sum = mirror_sum.reshape(n_blocks, feat_q, tile_dim).transpose(1, 0, 2)
    z_part = (local_sum + mirror_sum).reshape(feat_q, rows).astype(jnp.bfloat16)
    z_full = gather_groups(z_part, n_col)
    y_full = lax.dot_general(
        z_full, weight, (((0,), (0,)), ((), ())), preferred_element_type=jnp.float32
    )
    act = jax.nn.silu(y_full).astype(jnp.bfloat16)
    sig = jax.nn.sigmoid(y_full)
    grad_y = (cotangent.astype(jnp.float32) * sig * (1.0 + y_full * (1.0 - sig))).astype(
        jnp.bfloat16
    )
    grad_part = jnp.dot(z_part, grad_y, preferred_element_type=jnp.float32)
    grad_w = sum_over_row(grad_part, n_row)
    return (act, grad_w)


def solution(mesh):
    in_specs = (
        P("col", "row"),
        P("row", None, None),
        P("row", None),
        P("row", None),
        P(),
        P("row", None),
    )
    out_specs = (P("row", None), P("col", None))
    return jax.shard_map(body, mesh=mesh, in_specs=in_specs, out_specs=out_specs, check_vma=False)
```

profile of v0, /device:TPU:0, one launch (start us, length us, event | category | flops | bytes accessed | tf_op | source)
XLA Modules:
  0.0 63.9 jit_solution(13298071320299670246)
XLA Ops:
  0.6 0.8 %fusion.21 = s32[8,8]{1,0:T(8,128)S(1)} fusion(s32[8]{0:T(128)} %bitcast.82), kind=kLoop, calls=%fused_computation.46 | loop fusion | flops 128 | bytes 288 | tf_op jit(solution)/shard_map/convert_element_type | solution.py:44
  1.4 0.8 %select_reduce_fusion = s32[8]{0:T(128)S(1)} fusion(s32[8,8]{1,0:T(8,128)S(1)} %reduce_window_sum.11, s32[8]{0:T(128)} %bitcast.83), kind=kLoop, calls=%fused_computation.44 | loop fusion | flops 248 | bytes 320 | tf_op jit(solution)/shard_map/reduce_sum | solution.py:45
  2.3 0.8 %and_bitcast_fusion.1 = (pred[8]{0:T(512)(128)(4,1)S(1)}, s32[8,1]{0,1:T(1,128)S(1)}, pred[8]{0:T(512)(128)(4,1)S(1)}) fusion(s32[8,2]{0,1:T(2,128)} %param.11, s32[8,1]{0,1:T(1,128)} %param.10), kind=kLoop, calls=%fused_computation.63 | loop fusion | flops 112 | bytes 144 | tf_op jit(solution)/shard_map/jit(_take)/reduce_and | solution.py:68
  3.0 0.8 %slice_bitcast_fusion.2 = (s32[8]{0:T(128)S(1)}, s32[8]{0:T(128)S(1)}, s32[8]{0:T(128)S(1)}, s32[8]{0:T(128)S(1)}) fusion(s32[8,2]{0,1:T(2,128)} %param.11, s32[8]{0:T(128)S(1)} %select_reduce_fusion, s32[8,1]{0,1:T(1,128)} %param.10), kind=kLoop, calls=%fused_computation.72 | loop fusion | flops 64 | bytes 256 | tf_op jit(solution)/shard_map/eq | solution.py:73
  3.8 0.9 %bitcast_bitcast_fusion = (bf16[1,8,32,128]{3,2,1,0:T(8,128)(2,1)S(1)}, bf16[8,32,128]{2,1,0:T(8,128)(2,1)S(1)}) fusion(bf16[32,1024]{1,0:T(8,128)(2,1)} %param.8), kind=kLoop, calls=%fused_computation.28 | loop fusion | bytes 196608
  4.7 0.6 gather_fusion
  5.5 0.8 %scatter_custom_fusion = bf16[16,4096]{1,0:T(8,128)(2,1)S(1)} fusion(s32[8]{0:T(128)S(1)} %get-tuple-element.24, bf16[1,8,32,128]{3,2,1,0:T(8,128)(2,1)S(1)} %fusion.2, bf16[]{:T(256)} %constant.105.clone.1), kind=kCustom, calls=%fused_computation.24 | custom fusion | bytes 196610 | tf_op jit(solution)/shard_map/scatter | solution.py:59
  6.4 0.6 scatter_custom_fusion.1
  7.2 1.1 %fusion.3 = bf16[8,11,4096]{2,1,0:T(8,128)(2,1)} fusion(bf16[8,1,2]{2,1,0:T(2,128)(2,1)S(1)} %convert_element_type.72, bf16[8,2,4096]{2,1,0:T(2,128)(2,1)S(1)} %reshape.155, bf16[8,8,4096]{2,1,0:T(8,128)(2,1)S(1)} %broadcast_in_dim.53), kind=kLoop, calls=%fused_computation.11 | loop fusion | flops 2883584 | bytes 1376288 | tf_op jit(solution)/shard_map/concatenate | solution.py:63
  8.3 7.3 %all-to-all-start = ((bf16[8,11,4096]{2,1,0:T(8,128)(2,1)}), bf16[8,11,4096]{2,1,0:T(8,128)(2,1)S(1)}, u32[]{:S(2)}, u32[]{:S(2)}) async-start(bf16[8,11,4096]{2,1,0:T(8,128)(2,1)} %fusion.3), calls=%async_computation | async-start | bytes 2097152 | tf_op jit(solution)/shard_map/all_to_all | solution.py:64
  15.7 25.6 %all-to-all-done = bf16[8,11,4096]{2,1,0:T(8,128)(2,1)S(1)} async-done(((bf16[8,11,4096]{2,1,0:T(8,128)(2,1)}), bf16[8,11,4096]{2,1,0:T(8,128)(2,1)S(1)}, u32[]{:S(2)}, u32[]{:S(2)}) %all-to-all-start) | async-done | bytes 720928 | tf_op jit(solution)/shard_map/all_to_all | solution.py:64
  41.7 0.6 gather_fusion.1
  43.1 1.6 %collective-permute-start.1 = (bf16[32,1024]{1,0:T(8,128)(2,1)S(1)}, bf16[32,1024]{1,0:T(8,128)(2,1)S(1)}, u32[]{:S(2)}, u32[]{:S(2)}) collective-permute-start(bf16[32,1024]{1,0:T(8,128)(2,1)S(1)} %bitcast.77), channel_id=1, source_target_pairs={{0,2},{1,3},{2,0},{3,1},{4,6},{5,7},{6,4},{7,5},{8,10},{9,11},{10,... | collective-permute-start | bytes 196616 | tf_op jit(solution)/shard_map/ppermute | solution.py:14
  44.6 1.4 %collective-permute-start.2 = (bf16[32,1024]{1,0:T(8,128)(2,1)S(1)}, bf16[32,1024]{1,0:T(8,128)(2,1)S(1)}, u32[]{:S(2)}, u32[]{:S(2)}) collective-permute-start(bf16[32,1024]{1,0:T(8,128)(2,1)S(1)} %bitcast.78), channel_id=1, source_target_pairs={{0,3},{1,0},{2,1},{3,2},{4,7},{5,4},{6,5},{7,6},{8,11},{9,8},{10,9... | collective-permute-start | bytes 196616 | tf_op jit(solution)/shard_map/ppermute | solution.py:14
  46.0 0.8 %collective-permute-done = bf16[32,1024]{1,0:T(8,128)(2,1)S(1)} collective-permute-done((bf16[32,1024]{1,0:T(8,128)(2,1)S(1)}, bf16[32,1024]{1,0:T(8,128)(2,1)S(1)}, u32[]{:S(2)}, u32[]{:S(2)}) %collective-permute-start) | collective-permute-done | bytes 65568 | tf_op jit(solution)/shard_map/ppermute | solution.py:14
  46.8 0.9 %collective-permute-done.1 = bf16[32,1024]{1,0:T(8,128)(2,1)S(1)} collective-permute-done((bf16[32,1024]{1,0:T(8,128)(2,1)S(1)}, bf16[32,1024]{1,0:T(8,128)(2,1)S(1)}, u32[]{:S(2)}, u32[]{:S(2)}) %collective-permute-start.1) | collective-permute-done | bytes 65568 | tf_op jit(solution)/shard_map/ppermute | solution.py:14
  47.9 0.6 gather_fusion.2
  48.6 1.3 %multiply_convert_fusion.1 = (bf16[1024,256]{1,0:T(8,128)(2,1)}, f32[1024,256]{1,0:T(8,128)S(1)}) fusion(bf16[128,1024]{1,0:T(8,128)(2,1)S(1)} %bitcast_select_fusion, bf16[128,256]{1,0:T(8,128)(2,1)S(1)} %copy-done.2), kind=kOutput, calls=%fused_computation.13 | convolution fusion | flops 68419584 | bytes 1900544 | tf_op jit(solution)/shard_map/dot_general | solution.py:85
  49.9 0.5 fusion.4
  50.4 1.5 %collective-permute-start.3 = (f32[32,256]{1,0:T(8,128)S(1)}, f32[32,256]{1,0:T(8,128)S(1)}, u32[]{:S(2)}, u32[]{:S(2)}) collective-permute-start(f32[32,256]{1,0:T(8,128)S(1)} %fusion.4), channel_id=1, source_target_pairs={{0,4},{4,0},{8,12},{12,8},{16,20},{20,16},{24,28},{28,24},{1,5},{5... | collective-permute-start | bytes 98312 | tf_op jit(solution)/shard_map/ppermute | solution.py:27
  51.9 2.6 %collective-permute-done.3 = f32[32,256]{1,0:T(8,128)S(1)} collective-permute-done((f32[32,256]{1,0:T(8,128)S(1)}, f32[32,256]{1,0:T(8,128)S(1)}, u32[]{:S(2)}, u32[]{:S(2)}) %collective-permute-start.3) | collective-permute-done | bytes 32800 | tf_op jit(solution)/shard_map/ppermute | solution.py:27
  54.6 3.9 %collective-permute-done.4 = f32[32,256]{1,0:T(8,128)S(1)} collective-permute-done((f32[32,256]{1,0:T(8,128)S(1)}, f32[32,256]{1,0:T(8,128)S(1)}, u32[]{:S(2)}, u32[]{:S(2)}) %collective-permute-start.4) | collective-permute-done | bytes 32800 | tf_op jit(solution)/shard_map/ppermute | solution.py:27
  58.5 4.8 %collective-permute-done.5 = f32[32,256]{1,0:T(8,128)S(1)} collective-permute-done((f32[32,256]{1,0:T(8,128)S(1)}, f32[32,256]{1,0:T(8,128)S(1)}, u32[]{:S(2)}, u32[]{:S(2)}) %collective-permute-start.5) | collective-permute-done | bytes 32800 | tf_op jit(solution)/shard_map/ppermute | solution.py:27
  63.3 0.6 add.98
  (39 shorter events, 2.2 us)
Async XLA Ops:
  0.6 4.6 %copy-start = (bf16[8,128,128]{2,1,0:T(8,128)(2,1)S(1)}, bf16[8,128,128]{2,1,0:T(8,128)(2,1)}, u32[]{:S(2)}) copy-start(bf16[8,128,128]{2,1,0:T(8,128)(2,1)} %param.9) | copy-start | bytes 786436
  8.3 33.0 %all-to-all-start = ((bf16[8,11,4096]{2,1,0:T(8,128)(2,1)}), bf16[8,11,4096]{2,1,0:T(8,128)(2,1)S(1)}, u32[]{:S(2)}, u32[]{:S(2)}) async-start(bf16[8,11,4096]{2,1,0:T(8,128)(2,1)} %fusion.3), calls=%async_computation | async-start | bytes 2097152 | tf_op jit(solution)/shard_map/all_to_all | solution.py:64
  42.8 5.8 %copy-start.2 = (bf16[128,256]{1,0:T(8,128)(2,1)S(1)}, bf16[128,256]{1,0:T(8,128)(2,1)}, u32[]{:S(2)}) copy-start(bf16[128,256]{1,0:T(8,128)(2,1)} %param.12) | copy-start | bytes 196612
  43.0 3.8 %collective-permute-start = (bf16[32,1024]{1,0:T(8,128)(2,1)S(1)}, bf16[32,1024]{1,0:T(8,128)(2,1)S(1)}, u32[]{:S(2)}, u32[]{:S(2)}) collective-permute-start(bf16[32,1024]{1,0:T(8,128)(2,1)S(1)} %bitcast.76), channel_id=1, source_target_pairs={{0,1},{1,2},{2,3},{3,0},{4,5},{5,6},{6,7},{7,4},{8,9},{9,10},{10,1... | collective-permute-start | bytes 196616 | tf_op jit(solution)/shard_map/ppermute | solution.py:14
  43.1 4.6 %collective-permute-start.1 = (bf16[32,1024]{1,0:T(8,128)(2,1)S(1)}, bf16[32,1024]{1,0:T(8,128)(2,1)S(1)}, u32[]{:S(2)}, u32[]{:S(2)}) collective-permute-start(bf16[32,1024]{1,0:T(8,128)(2,1)S(1)} %bitcast.77), channel_id=1, source_target_pairs={{0,2},{1,3},{2,0},{3,1},{4,6},{5,7},{6,4},{7,5},{8,10},{9,11},{10,... | collective-permute-start | bytes 196616 | tf_op jit(solution)/shard_map/ppermute | solution.py:14
  44.6 3.3 %collective-permute-start.2 = (bf16[32,1024]{1,0:T(8,128)(2,1)S(1)}, bf16[32,1024]{1,0:T(8,128)(2,1)S(1)}, u32[]{:S(2)}, u32[]{:S(2)}) collective-permute-start(bf16[32,1024]{1,0:T(8,128)(2,1)S(1)} %bitcast.78), channel_id=1, source_target_pairs={{0,3},{1,0},{2,1},{3,2},{4,7},{5,4},{6,5},{7,6},{8,11},{9,8},{10,9... | collective-permute-start | bytes 196616 | tf_op jit(solution)/shard_map/ppermute | solution.py:14
  48.6 1.3 %copy-start.1 = (bf16[1024,256]{1,0:T(8,128)(2,1)S(1)}, bf16[1024,256]{1,0:T(8,128)(2,1)}, u32[]{:S(2)}) copy-start(bf16[1024,256]{1,0:T(8,128)(2,1)} %param.13) | copy-start | bytes 1572868
  50.4 4.1 %collective-permute-start.3 = (f32[32,256]{1,0:T(8,128)S(1)}, f32[32,256]{1,0:T(8,128)S(1)}, u32[]{:S(2)}, u32[]{:S(2)}) collective-permute-start(f32[32,256]{1,0:T(8,128)S(1)} %fusion.4), channel_id=1, source_target_pairs={{0,4},{4,0},{8,12},{12,8},{16,20},{20,16},{24,28},{28,24},{1,5},{5... | collective-permute-start | bytes 98312 | tf_op jit(solution)/shard_map/ppermute | solution.py:27
  54.6 3.9 %collective-permute-start.4 = (f32[32,256]{1,0:T(8,128)S(1)}, f32[32,256]{1,0:T(8,128)S(1)}, u32[]{:S(2)}, u32[]{:S(2)}) collective-permute-start(f32[32,256]{1,0:T(8,128)S(1)} %add.96), channel_id=1, source_target_pairs={{0,8},{4,12},{8,0},{12,4},{16,24},{20,28},{24,16},{28,20},{1,9},{5... | collective-permute-start | bytes 98312 | tf_op jit(solution)/shard_map/ppermute | solution.py:27
  58.5 4.8 %collective-permute-start.5 = (f32[32,256]{1,0:T(8,128)S(1)}, f32[32,256]{1,0:T(8,128)S(1)}, u32[]{:S(2)}, u32[]{:S(2)}) collective-permute-start(f32[32,256]{1,0:T(8,128)S(1)} %add.97), channel_id=1, source_target_pairs={{0,16},{4,20},{8,24},{12,28},{16,0},{20,4},{24,8},{28,12},{1,17},{... | collective-permute-start | bytes 98312 | tf_op jit(solution)/shard_map/ppermute | solution.py:27
where the time goes:
time: 64.2 us; the launch traced here: 63.9 us
  waiting for transfers between devices  38.8 us (60%)
  starting transfers between devices  11.8 us (18%)
  other arithmetic  5.09 us (8%)
  local copies, waits for them, and re-layouts  4.72 us (7%)
  matrix products  2.72 us (4%)
  between operations  0.86 us (1%)
    all_to_all x1, waiting for transfers between devices, body(): lax.all_to_all(payload, 'row', split_axis=0, concat_axis=0, tiled=True)  25.6 us
    ppermute x3, waiting for transfers between devices, sum_over_row(): x = x + lax.ppermute(x, 'row', perm)  11.3 us
    all_to_all x1, starting transfers between devices, body(): lax.all_to_all(payload, 'row', split_axis=0, concat_axis=0, tiled=True)  7.28 us
    ppermute x3, starting transfers between devices, gather_groups(): parts.append(lax.ppermute(z_part, 'col', perm))  3 us
    ppermute x3, waiting for transfers between devices, gather_groups(): parts.append(lax.ppermute(z_part, 'col', perm))  1.86 us
    ppermute x3, starting transfers between devices, sum_over_row(): x = x + lax.ppermute(x, 'row', perm)  1.49 us
  transfers between devices with their start and end apart: 7, of which 7 were waited for; matrix products, arithmetic and copies ran while one was open for 0% of the time, Pallas kernels for 0%

commit v1 on v0

--- a/solution.py
+++ b/solution.py
@@ -2,6 +2,17 @@
 import jax.numpy as jnp
 from jax import lax
 from jax.sharding import PartitionSpec as P
+
+
+def in_blocks(x, dim, size):
+    before, after = (x.shape[:dim], x.shape[dim + 1 :])
+    return jnp.moveaxis(x.reshape(*before, size, -1, *after), dim, 0)
+
+
+def joined_along(tiles, dim):
+    lengths = list(tiles.shape[1:])
+    lengths[dim] *= tiles.shape[0]
+    return jnp.moveaxis(tiles, 0, dim).reshape(lengths)
 
 
 def gather_groups(z_part, n_col):
@@ -61,7 +72,14 @@
     )
     every_block = jnp.broadcast_to(flat_blocks[None], (n_row, n_blocks, feat_q * tile_dim))
     payload = jnp.concatenate([every_block, outgoing, id_rows], axis=1)
-    got = lax.all_to_all(payload, "row", split_axis=0, concat_axis=0, tiled=True)
+    peers, here = (lax.axis_size("row"), lax.axis_index("row"))
+    blocks = in_blocks(payload, 0, peers)
+    outs = [blocks[here]]
+    for step in range(1, peers):
+        sent = blocks[here ^ step]
+        outs.append(lax.ppermute(sent, "row", [(i_2, i_2 ^ step) for i_2 in range(peers)]))
+    blocks = jnp.stack(outs)[here ^ jnp.arange(peers)]
+    got = joined_along(blocks, 0)
     all_x = got[:, :n_blocks].reshape(n_row * n_blocks, feat_q, tile_dim)
     incoming = got[:, n_blocks : n_blocks + capacity]
     block_ids = got[:, n_blocks + capacity, :capacity].astype(jnp.int32)

time: 64.2 us -> 62.2 us (0.969)
  waiting for transfers between devices: 38.8 us -> 19.6 us
  starting transfers between devices: 11.8 us -> 25.2 us
  local copies, waits for them, and re-layouts: 4.72 us -> 8.22 us
    all_to_all x1 -> x0, waiting for transfers between devices: 25.6 us -> none  [body(): lax.all_to_all(payload, 'row', split_axis=0, concat_axis=0, tiled=True)]
    ppermute x0 -> x7, starting transfers between devices: none -> 12.8 us  [body(): lax.ppermute(sent, 'row', [(i_2, i_2 ^ step) for i_2 in range(peers)])]
    ppermute x0 -> x7, waiting for transfers between devices: none -> 10.7 us  [body(): lax.ppermute(sent, 'row', [(i_2, i_2 ^ step) for i_2 in range(peers)])]
    ppermute x3, starting transfers between devices: 1.49 us -> 9.32 us  [sum_over_row(): x = x + lax.ppermute(x, 'row', perm)]
    all_to_all x1 -> x0, starting transfers between devices: 7.28 us -> none  [body(): lax.all_to_all(payload, 'row', split_axis=0, concat_axis=0, tiled=True)]
    ppermute x3, waiting for transfers between devices: 11.3 us -> 7.12 us  [sum_over_row(): x = x + lax.ppermute(x, 'row', perm)]
    unnamed x11 -> x22, local copies, waits for them, and re-layouts: 1.05 us -> 3.84 us
    concatenate x1, other arithmetic: 1.1 us -> 0.13 us  [body(): payload = jnp.concatenate([every_block, outgoing, id_rows], axis=1)]
  transfers between devices with their start and end apart: 7 -> 13, of which waited for: 7 -> 7; matrix products, arithmetic and copies ran while one was open for 0% -> 6% of each run, Pallas kernels for 0% -> 0%
where the time goes in v1:
time: 62.2 us; the launch traced here: 61.9 us
  starting transfers between devices  25.2 us (41%)
  waiting for transfers between devices  19.6 us (32%)
  local copies, waits for them, and re-layouts  8.22 us (13%)
  other arithmetic  5.15 us (8%)
  matrix products  2.72 us (4%)
  between operations  1.06 us (2%)
    ppermute x7, starting transfers between devices, body(): lax.ppermute(sent, 'row', [(i_2, i_2 ^ step) for i_2 in range(peers)])  12.8 us
    ppermute x7, waiting for transfers between devices, body(): lax.ppermute(sent, 'row', [(i_2, i_2 ^ step) for i_2 in range(peers)])  10.7 us
    ppermute x3, starting transfers between devices, sum_over_row(): x = x + lax.ppermute(x, 'row', perm)  9.32 us
    ppermute x3, waiting for transfers between devices, sum_over_row(): x = x + lax.ppermute(x, 'row', perm)  7.12 us
    unnamed x22, local copies, waits for them, and re-layouts  3.84 us
    ppermute x3, starting transfers between devices, gather_groups(): parts.append(lax.ppermute(z_part, 'col', perm))  3 us
    ppermute x3, waiting for transfers between devices, gather_groups(): parts.append(lax.ppermute(z_part, 'col', perm))  1.85 us
    reduce_and x1, other arithmetic, body(): fetched_tiles = jnp.take(all_x, owner * n_blocks + col_local, axis=0)  1.28 us
  transfers between devices with their start and end apart: 13, of which 7 were waited for; matrix products, arithmetic and copies ran while one was open for 6% of the time, Pallas kernels for 0%

profile of v1, /device:TPU:0, one launch (start us, length us, event | category | flops | bytes accessed | tf_op | source)
XLA Modules:
  0.0 61.9 jit_solution(15660003803200795951)
XLA Ops:
  0.7 0.8 %fusion.21 = s32[8,8]{1,0:T(8,128)S(1)} fusion(s32[8]{0:T(128)} %bitcast.114), kind=kLoop, calls=%fused_computation.56 | loop fusion | flops 128 | bytes 288 | tf_op jit(solution)/shard_map/convert_element_type | solution.py:55
  1.5 0.8 %select_reduce_fusion = s32[8]{0:T(128)S(1)} fusion(s32[8,8]{1,0:T(8,128)S(1)} %reduce_window_sum.11, s32[8]{0:T(128)} %bitcast.115), kind=kLoop, calls=%fused_computation.54 | loop fusion | flops 248 | bytes 320 | tf_op jit(solution)/shard_map/reduce_sum | solution.py:56
  2.3 1.3 %and_bitcast_fusion.1 = (pred[8]{0:T(512)(128)(4,1)}, s32[8,1]{0,1:T(1,128)S(1)}, pred[8]{0:T(512)(128)(4,1)S(1)}) fusion(s32[8,2]{0,1:T(2,128)} %param.11, s32[8,1]{0,1:T(1,128)} %param.10), kind=kLoop, calls=%fused_computation.81 | loop fusion | flops 112 | bytes 144 | tf_op jit(solution)/shard_map/jit(_take)/reduce_and | solution.py:86
  4.3 0.9 %bitcast_bitcast_fusion = (bf16[1,8,32,128]{3,2,1,0:T(8,128)(2,1)S(1)}, bf16[8,32,128]{2,1,0:T(8,128)(2,1)S(1)}) fusion(bf16[32,1024]{1,0:T(8,128)(2,1)} %param.8), kind=kLoop, calls=%fused_computation.37 | loop fusion | bytes 196608
  7.9 3.0 %collective-permute-start = (bf16[1,11,4096]{2,1,0:T(8,128)(2,1)S(1)}, bf16[1,11,4096]{2,1,0:T(8,128)(2,1)}, u32[]{:S(2)}, u32[]{:S(2)}) collective-permute-start(bf16[1,11,4096]{2,1,0:T(8,128)(2,1)S(1)} %get-tuple-element.22), channel_id=1, source_target_pairs={{0,4},{4,0},{8,12},{12,8},{16,20},{20,16},{24,28},{28,24},{1,5},{5... | collective-permute-start | bytes 270344 | tf_op jit(solution)/shard_map/ppermute | solution.py:80
  11.0 1.6 %collective-permute-start.1 = (bf16[1,11,4096]{2,1,0:T(8,128)(2,1)S(1)}, bf16[1,11,4096]{2,1,0:T(8,128)(2,1)}, u32[]{:S(2)}, u32[]{:S(2)}) collective-permute-start(bf16[1,11,4096]{2,1,0:T(8,128)(2,1)S(1)} %get-tuple-element.21), channel_id=1, source_target_pairs={{0,8},{4,12},{8,0},{12,4},{16,24},{20,28},{24,16},{28,20},{1,9},{5... | collective-permute-start | bytes 270344 | tf_op jit(solution)/shard_map/ppermute | solution.py:80
  12.6 3.0 %collective-permute-start.3 = (bf16[1,11,4096]{2,1,0:T(8,128)(2,1)S(1)}, bf16[1,11,4096]{2,1,0:T(8,128)(2,1)S(1)}, u32[]{:S(2)}, u32[]{:S(2)}) collective-permute-start(bf16[1,11,4096]{2,1,0:T(8,128)(2,1)S(1)} %get-tuple-element.19), channel_id=1, source_target_pairs={{0,16},{4,20},{8,24},{12,28},{16,0},{20,4},{24,8},{28,12},{1,17},{... | collective-permute-start | bytes 270344 | tf_op jit(solution)/shard_map/ppermute | solution.py:80
  15.5 1.3 %collective-permute-start.4 = (bf16[1,11,4096]{2,1,0:T(8,128)(2,1)S(1)}, bf16[1,11,4096]{2,1,0:T(8,128)(2,1)S(1)}, u32[]{:S(2)}, u32[]{:S(2)}) collective-permute-start(bf16[1,11,4096]{2,1,0:T(8,128)(2,1)S(1)} %get-tuple-element.18), channel_id=1, source_target_pairs={{0,20},{4,16},{8,28},{12,24},{16,4},{20,0},{24,12},{28,8},{1,21},{... | collective-permute-start | bytes 270344 | tf_op jit(solution)/shard_map/ppermute | solution.py:80
  17.6 3.6 %collective-permute-start.5 = (bf16[1,11,4096]{2,1,0:T(8,128)(2,1)S(1)}, bf16[1,11,4096]{2,1,0:T(8,128)(2,1)S(1)}, u32[]{:S(2)}, u32[]{:S(2)}) collective-permute-start(bf16[1,11,4096]{2,1,0:T(8,128)(2,1)S(1)} %get-tuple-element.17), channel_id=1, source_target_pairs={{0,24},{4,28},{8,16},{12,20},{16,8},{20,12},{24,0},{28,4},{1,25},{... | collective-permute-start | bytes 270344 | tf_op jit(solution)/shard_map/ppermute | solution.py:80
  21.2 0.9 %bitcast_dynamic-update-slice_fusion.5 = bf16[8,1,11,4096]{3,2,0,1:T(8,128)(2,1)S(1)} fusion(bf16[8,1,11,4096]{3,2,0,1:T(8,128)(2,1)S(1)} %bitcast_dynamic-update-slice_fusion.7, bf16[1,11,4096]{2,1,0:T(8,128)(2,1)} %collective-permute-done), kind=kLoop, calls=%fused_computation.27 | loop fusion | bytes 221184
  22.5 0.9 %bitcast_dynamic-update-slice_fusion.4 = bf16[8,1,11,4096]{3,2,0,1:T(8,128)(2,1)S(1)} fusion(bf16[8,1,11,4096]{3,2,0,1:T(8,128)(2,1)S(1)} %bitcast_dynamic-update-slice_fusion.5, bf16[1,11,4096]{2,1,0:T(8,128)(2,1)} %collective-permute-done.1), kind=kLoop, calls=%fused_computation.26 | loop fusion | bytes 221184
  23.4 0.9 %bitcast_dynamic-update-slice_fusion.3 = bf16[8,1,11,4096]{3,2,0,1:T(8,128)(2,1)S(1)} fusion(bf16[8,1,11,4096]{3,2,0,1:T(8,128)(2,1)S(1)} %bitcast_dynamic-update-slice_fusion.4, bf16[1,11,4096]{2,1,0:T(8,128)(2,1)} %collective-permute-done.2), kind=kLoop, calls=%fused_computation.25 | loop fusion | bytes 221184
  24.4 10.6 %collective-permute-done.4 = bf16[1,11,4096]{2,1,0:T(8,128)(2,1)S(1)} collective-permute-done((bf16[1,11,4096]{2,1,0:T(8,128)(2,1)S(1)}, bf16[1,11,4096]{2,1,0:T(8,128)(2,1)S(1)}, u32[]{:S(2)}, u32[]{:S(2)}) %collective-permute-start.4) | collective-permute-done | bytes 90144 | tf_op jit(solution)/shard_map/ppermute | solution.py:80
  37.5 1.6 %collective-permute-start.8 = (bf16[32,1024]{1,0:T(8,128)(2,1)S(1)}, bf16[32,1024]{1,0:T(8,128)(2,1)S(1)}, u32[]{:S(2)}, u32[]{:S(2)}) collective-permute-start(bf16[32,1024]{1,0:T(8,128)(2,1)S(1)} %bitcast.109), channel_id=1, source_target_pairs={{0,2},{1,3},{2,0},{3,1},{4,6},{5,7},{6,4},{7,5},{8,10},{9,11},{10,... | collective-permute-start | bytes 196616 | tf_op jit(solution)/shard_map/ppermute | solution.py:25
  39.0 1.4 %collective-permute-start.9 = (bf16[32,1024]{1,0:T(8,128)(2,1)S(1)}, bf16[32,1024]{1,0:T(8,128)(2,1)S(1)}, u32[]{:S(2)}, u32[]{:S(2)}) collective-permute-start(bf16[32,1024]{1,0:T(8,128)(2,1)S(1)} %bitcast.110), channel_id=1, source_target_pairs={{0,3},{1,0},{2,1},{3,2},{4,7},{5,4},{6,5},{7,6},{8,11},{9,8},{10,9... | collective-permute-start | bytes 196616 | tf_op jit(solution)/shard_map/ppermute | solution.py:25
  40.5 0.8 %collective-permute-done.7 = bf16[32,1024]{1,0:T(8,128)(2,1)S(1)} collective-permute-done((bf16[32,1024]{1,0:T(8,128)(2,1)S(1)}, bf16[32,1024]{1,0:T(8,128)(2,1)S(1)}, u32[]{:S(2)}, u32[]{:S(2)}) %collective-permute-start.7) | collective-permute-done | bytes 65568 | tf_op jit(solution)/shard_map/ppermute | solution.py:25
  41.2 0.9 %collective-permute-done.8 = bf16[32,1024]{1,0:T(8,128)(2,1)S(1)} collective-permute-done((bf16[32,1024]{1,0:T(8,128)(2,1)S(1)}, bf16[32,1024]{1,0:T(8,128)(2,1)S(1)}, u32[]{:S(2)}, u32[]{:S(2)}) %collective-permute-start.8) | collective-permute-done | bytes 65568 | tf_op jit(solution)/shard_map/ppermute | solution.py:25
  43.1 1.3 %multiply_convert_fusion.1 = (bf16[1024,256]{1,0:T(8,128)(2,1)}, f32[1024,256]{1,0:T(8,128)S(1)}) fusion(bf16[128,1024]{1,0:T(8,128)(2,1)S(1)} %bitcast_select_fusion, bf16[128,256]{1,0:T(8,128)(2,1)S(1)} %copy-done.4), kind=kOutput, calls=%fused_computation.14 | convolution fusion | flops 68419584 | bytes 1900544 | tf_op jit(solution)/shard_map/dot_general | solution.py:103
  44.9 0.8 %collective-permute-start.10 = (f32[32,256]{1,0:T(8,128)S(1)}, f32[32,256]{1,0:T(8,128)S(1)}, u32[]{:S(2)}, u32[]{:S(2)}) collective-permute-start(f32[32,256]{1,0:T(8,128)S(1)} %fusion.4), channel_id=1, source_target_pairs={{0,4},{4,0},{8,12},{12,8},{16,20},{20,16},{24,28},{28,24},{1,5},{5... | collective-permute-start | bytes 98312 | tf_op jit(solution)/shard_map/ppermute | solution.py:38
  45.6 3.3 %collective-permute-done.10 = f32[32,256]{1,0:T(8,128)S(1)} collective-permute-done((f32[32,256]{1,0:T(8,128)S(1)}, f32[32,256]{1,0:T(8,128)S(1)}, u32[]{:S(2)}, u32[]{:S(2)}) %collective-permute-start.10) | collective-permute-done | bytes 32800 | tf_op jit(solution)/shard_map/ppermute | solution.py:38
  49.0 5.0 %collective-permute-start.11 = (f32[32,256]{1,0:T(8,128)S(1)}, f32[32,256]{1,0:T(8,128)S(1)}, u32[]{:S(2)}, u32[]{:S(2)}) collective-permute-start(f32[32,256]{1,0:T(8,128)S(1)} %add.139), channel_id=1, source_target_pairs={{0,8},{4,12},{8,0},{12,4},{16,24},{20,28},{24,16},{28,20},{1,9},{5... | collective-permute-start | bytes 98312 | tf_op jit(solution)/shard_map/ppermute | solution.py:38
  54.0 1.9 %collective-permute-done.11 = f32[32,256]{1,0:T(8,128)S(1)} collective-permute-done((f32[32,256]{1,0:T(8,128)S(1)}, f32[32,256]{1,0:T(8,128)S(1)}, u32[]{:S(2)}, u32[]{:S(2)}) %collective-permute-start.11) | collective-permute-done | bytes 32800 | tf_op jit(solution)/shard_map/ppermute | solution.py:38
  55.9 3.5 %collective-permute-start.12 = (f32[32,256]{1,0:T(8,128)S(1)}, f32[32,256]{1,0:T(8,128)S(1)}, u32[]{:S(2)}, u32[]{:S(2)}) collective-permute-start(f32[32,256]{1,0:T(8,128)S(1)} %add.140), channel_id=1, source_target_pairs={{0,16},{4,20},{8,24},{12,28},{16,0},{20,4},{24,8},{28,12},{1,17},{... | collective-permute-start | bytes 98312 | tf_op jit(solution)/shard_map/ppermute | solution.py:38
  59.4 1.9 %collective-permute-done.12 = f32[32,256]{1,0:T(8,128)S(1)} collective-permute-done((f32[32,256]{1,0:T(8,128)S(1)}, f32[32,256]{1,0:T(8,128)S(1)}, u32[]{:S(2)}, u32[]{:S(2)}) %collective-permute-start.12) | collective-permute-done | bytes 32800 | tf_op jit(solution)/shard_map/ppermute | solution.py:38
  (67 shorter events, 9.0 us)
Async XLA Ops:
  0.6 5.1 %copy-start = (bf16[8,128,128]{2,1,0:T(8,128)(2,1)S(1)}, bf16[8,128,128]{2,1,0:T(8,128)(2,1)}, u32[]{:S(2)}) copy-start(bf16[8,128,128]{2,1,0:T(8,128)(2,1)} %param.9) | copy-start | bytes 786436
  7.9 9.6 %collective-permute-start = (bf16[1,11,4096]{2,1,0:T(8,128)(2,1)S(1)}, bf16[1,11,4096]{2,1,0:T(8,128)(2,1)}, u32[]{:S(2)}, u32[]{:S(2)}) collective-permute-start(bf16[1,11,4096]{2,1,0:T(8,128)(2,1)S(1)} %get-tuple-element.22), channel_id=1, source_target_pairs={{0,4},{4,0},{8,12},{12,8},{16,20},{20,16},{24,28},{28,24},{1,5},{5... | collective-permute-start | bytes 270344 | tf_op jit(solution)/shard_map/ppermute | solution.py:80
  11.0 11.1 %collective-permute-start.1 = (bf16[1,11,4096]{2,1,0:T(8,128)(2,1)S(1)}, bf16[1,11,4096]{2,1,0:T(8,128)(2,1)}, u32[]{:S(2)}, u32[]{:S(2)}) collective-permute-start(bf16[1,11,4096]{2,1,0:T(8,128)(2,1)S(1)} %get-tuple-element.21), channel_id=1, source_target_pairs={{0,8},{4,12},{8,0},{12,4},{16,24},{20,28},{24,16},{28,20},{1,9},{5... | collective-permute-start | bytes 270344 | tf_op jit(solution)/shard_map/ppermute | solution.py:80
  12.6 10.8 %collective-permute-start.2 = (bf16[1,11,4096]{2,1,0:T(8,128)(2,1)S(1)}, bf16[1,11,4096]{2,1,0:T(8,128)(2,1)}, u32[]{:S(2)}, u32[]{:S(2)}) collective-permute-start(bf16[1,11,4096]{2,1,0:T(8,128)(2,1)S(1)} %get-tuple-element.20), channel_id=1, source_target_pairs={{0,12},{4,8},{8,4},{12,0},{16,28},{20,24},{24,20},{28,16},{1,13},{... | collective-permute-start | bytes 270344 | tf_op jit(solution)/shard_map/ppermute | solution.py:80
  12.6 11.8 %collective-permute-start.3 = (bf16[1,11,4096]{2,1,0:T(8,128)(2,1)S(1)}, bf16[1,11,4096]{2,1,0:T(8,128)(2,1)S(1)}, u32[]{:S(2)}, u32[]{:S(2)}) collective-permute-start(bf16[1,11,4096]{2,1,0:T(8,128)(2,1)S(1)} %get-tuple-element.19), channel_id=1, source_target_pairs={{0,16},{4,20},{8,24},{12,28},{16,0},{20,4},{24,8},{28,12},{1,17},{... | collective-permute-start | bytes 270344 | tf_op jit(solution)/shard_map/ppermute | solution.py:80
  15.5 19.4 %collective-permute-start.4 = (bf16[1,11,4096]{2,1,0:T(8,128)(2,1)S(1)}, bf16[1,11,4096]{2,1,0:T(8,128)(2,1)S(1)}, u32[]{:S(2)}, u32[]{:S(2)}) collective-permute-start(bf16[1,11,4096]{2,1,0:T(8,128)(2,1)S(1)} %get-tuple-element.18), channel_id=1, source_target_pairs={{0,20},{4,16},{8,28},{12,24},{16,4},{20,0},{24,12},{28,8},{1,21},{... | collective-permute-start | bytes 270344 | tf_op jit(solution)/shard_map/ppermute | solution.py:80
  17.6 17.4 %collective-permute-start.5 = (bf16[1,11,4096]{2,1,0:T(8,128)(2,1)S(1)}, bf16[1,11,4096]{2,1,0:T(8,128)(2,1)S(1)}, u32[]{:S(2)}, u32[]{:S(2)}) collective-permute-start(bf16[1,11,4096]{2,1,0:T(8,128)(2,1)S(1)} %get-tuple-element.17), channel_id=1, source_target_pairs={{0,24},{4,28},{8,16},{12,20},{16,8},{20,12},{24,0},{28,4},{1,25},{... | collective-permute-start | bytes 270344 | tf_op jit(solution)/shard_map/ppermute | solution.py:80
  22.1 12.9 %collective-permute-start.6 = (bf16[1,11,4096]{2,1,0:T(8,128)(2,1)S(1)}, bf16[1,11,4096]{2,1,0:T(8,128)(2,1)S(1)}, u32[]{:S(2)}, u32[]{:S(2)}) collective-permute-start(bf16[1,11,4096]{2,1,0:T(8,128)(2,1)S(1)} %get-tuple-element.16), channel_id=1, source_target_pairs={{0,28},{4,24},{8,20},{12,16},{16,12},{20,8},{24,4},{28,0},{1,29},{... | collective-permute-start | bytes 270344 | tf_op jit(solution)/shard_map/ppermute | solution.py:80
  35.7 0.9 %copy-start.1 = (pred[8]{0:T(512)(128)(4,1)S(1)}, pred[8]{0:T(512)(128)(4,1)}, u32[]{:S(2)}) copy-start(pred[8]{0:T(512)(128)(4,1)} %get-tuple-element.14) | copy-start | bytes 28
  35.9 4.5 %copy-start.2 = (s32[4]{0:T(128)S(1)}, s32[4]{0:T(128)}, u32[]{:S(2)}) copy-start(s32[4]{0:T(128)} %fusion.32) | copy-start | bytes 52
  37.2 5.8 %copy-start.4 = (bf16[128,256]{1,0:T(8,128)(2,1)S(1)}, bf16[128,256]{1,0:T(8,128)(2,1)}, u32[]{:S(2)}) copy-start(bf16[128,256]{1,0:T(8,128)(2,1)} %param.12) | copy-start | bytes 196612
  37.4 3.8 %collective-permute-start.7 = (bf16[32,1024]{1,0:T(8,128)(2,1)S(1)}, bf16[32,1024]{1,0:T(8,128)(2,1)S(1)}, u32[]{:S(2)}, u32[]{:S(2)}) collective-permute-start(bf16[32,1024]{1,0:T(8,128)(2,1)S(1)} %bitcast.108), channel_id=1, source_target_pairs={{0,1},{1,2},{2,3},{3,0},{4,5},{5,6},{6,7},{7,4},{8,9},{9,10},{10,1... | collective-permute-start | bytes 196616 | tf_op jit(solution)/shard_map/ppermute | solution.py:25
  37.5 4.6 %collective-permute-start.8 = (bf16[32,1024]{1,0:T(8,128)(2,1)S(1)}, bf16[32,1024]{1,0:T(8,128)(2,1)S(1)}, u32[]{:S(2)}, u32[]{:S(2)}) collective-permute-start(bf16[32,1024]{1,0:T(8,128)(2,1)S(1)} %bitcast.109), channel_id=1, source_target_pairs={{0,2},{1,3},{2,0},{3,1},{4,6},{5,7},{6,4},{7,5},{8,10},{9,11},{10,... | collective-permute-start | bytes 196616 | tf_op jit(solution)/shard_map/ppermute | solution.py:25
  39.0 3.3 %collective-permute-start.9 = (bf16[32,1024]{1,0:T(8,128)(2,1)S(1)}, bf16[32,1024]{1,0:T(8,128)(2,1)S(1)}, u32[]{:S(2)}, u32[]{:S(2)}) collective-permute-start(bf16[32,1024]{1,0:T(8,128)(2,1)S(1)} %bitcast.110), channel_id=1, source_target_pairs={{0,3},{1,0},{2,1},{3,2},{4,7},{5,4},{6,5},{7,6},{8,11},{9,8},{10,9... | collective-permute-start | bytes 196616 | tf_op jit(solution)/shard_map/ppermute | solution.py:25
  43.0 1.3 %copy-start.3 = (bf16[1024,256]{1,0:T(8,128)(2,1)S(1)}, bf16[1024,256]{1,0:T(8,128)(2,1)}, u32[]{:S(2)}) copy-start(bf16[1024,256]{1,0:T(8,128)(2,1)} %param.13) | copy-start | bytes 1572868
  44.9 4.1 %collective-permute-start.10 = (f32[32,256]{1,0:T(8,128)S(1)}, f32[32,256]{1,0:T(8,128)S(1)}, u32[]{:S(2)}, u32[]{:S(2)}) collective-permute-start(f32[32,256]{1,0:T(8,128)S(1)} %fusion.4), channel_id=1, source_target_pairs={{0,4},{4,0},{8,12},{12,8},{16,20},{20,16},{24,28},{28,24},{1,5},{5... | collective-permute-start | bytes 98312 | tf_op jit(solution)/shard_map/ppermute | solution.py:38
  49.0 6.9 %collective-permute-start.11 = (f32[32,256]{1,0:T(8,128)S(1)}, f32[32,256]{1,0:T(8,128)S(1)}, u32[]{:S(2)}, u32[]{:S(2)}) collective-permute-start(f32[32,256]{1,0:T(8,128)S(1)} %add.139), channel_id=1, source_target_pairs={{0,8},{4,12},{8,0},{12,4},{16,24},{20,28},{24,16},{28,20},{1,9},{5... | collective-permute-start | bytes 98312 | tf_op jit(solution)/shard_map/ppermute | solution.py:38
  55.9 5.4 %collective-permute-start.12 = (f32[32,256]{1,0:T(8,128)S(1)}, f32[32,256]{1,0:T(8,128)S(1)}, u32[]{:S(2)}, u32[]{:S(2)}) collective-permute-start(f32[32,256]{1,0:T(8,128)S(1)} %add.140), channel_id=1, source_target_pairs={{0,16},{4,20},{8,24},{12,28},{16,0},{20,4},{24,8},{28,12},{1,17},{... | collective-permute-start | bytes 98312 | tf_op jit(solution)/shard_map/ppermute | solution.py:38
